TPU v7x, 256 devices: a whole 4x4x8 slice. The times are simulated.
256 devices in a mesh: sec: 2 (over y_lo), dp: 8 (over x, y_hi), seq: 16 (over z, core).
Axes of the slice: x: 4, y: 4 (y_hi: 2, y_lo: 2; y = y_hi * 2 + y_lo), z: 8, core: 2. Of those that a mesh axis runs over, the one named last changes fastest.
Arguments:
- hidden: bfloat16 [256, 128, 2560], P(('sec', 'dp', 'seq')), may hold values from -24 to 24
- cond_shift: bfloat16 [256, 2560], P(('sec', 'dp', 'seq')), may hold values from -0.3125 to 0.3125
- cond_scale: bfloat16 [256, 2560], P(('sec', 'dp', 'seq')), may hold values from -1.75 to 1.75
- noisy: bfloat16 [256, 128, 256], P(('sec', 'dp', 'seq')), may hold values from -6 to 6
- noise_level: float32 [256], P(('sec', 'dp', 'seq')), may hold values from 0.2 to 1
- w_out: bfloat16 [2560, 256], replicated, may hold values from -0.125 to 0.125
- w_embed: bfloat16 [256, 2048], replicated, may hold values from -0.375 to 0.375
- w_root: bfloat16 [2, 2048], replicated, may hold values from -0.03125 to 0.03125
- w_qkv: bfloat16 [3, 2048, 2048], P(None, None, 'seq'), may hold values from -0.125 to 0.125
- w_proj: bfloat16 [2048, 512], P('seq'), may hold values from -0.125 to 0.125
- text_table: bfloat16 [49408, 512], P('seq'), may hold values from -6 to 6
- text_ids: int32 [32, 32], replicated, may hold values from 0 to 49407
- prompt_index: int32 [256], P(('sec', 'dp')), may hold values from 0 to 31
- reward_weight: float32 [256], P(('sec', 'dp')), may hold values from 1000 to 4000
Outputs:
- rewards: float32 [256], P(('sec', 'dp'))
- grad_w_out: float32 [2560, 256], P('seq')
- grad_hidden: bfloat16 [256, 128, 2560], P(('sec', 'dp', 'seq'))
All inputs are finite; a program needn't handle non-finite values.
Results may differ from a plain program's by a relative error of at most 0.017.
The roundings to bfloat16 on the way count: a program that leaves them out, or rounds other values in their place, can miss the bound.
Values may be sent and summed in bfloat16 or wider, within the bound.
No kernel may reach another device: no remote copies, remote signals or barrier semaphores. Data moves between devices by JAX's collectives and lax.ppermute only.
A program may use at most 128 MiB of HBM per device.

v0:
```python
import jax
import jax.numpy as jnp
from jax import lax
from jax.sharding import PartitionSpec as P

D_REW = 2048
HEADS = 16
PROMPTS = 32
normalizing_sharpness = 10.0
epsilon = 1e-06
highest = lax.Precision.HIGHEST


def rotate(angle, first, second):
    cosine = jnp.cos(angle)
    sine_term = jnp.sin(angle)
    return (cosine * first + sine_term * second, cosine * second - sine_term * first)


def suffix(values):
    return jnp.sum(values, axis=1, keepdims=True) - jnp.cumsum(values, axis=1)


def local_path(motion):
    spin = motion[..., 0]
    theta = jnp.cumsum(spin, axis=1) - spin
    step_east, step_north = rotate(theta, motion[..., 1], motion[..., 2])
    path_east = jnp.cumsum(step_east, axis=1) - step_east
    path_north = jnp.cumsum(step_north, axis=1) - step_north
    return (theta, path_east, path_north)


def embed(motion, root_east, root_north, w_embed, root_rows):
    emb = jnp.einsum(
        "cfe,ed->cfd", motion.astype(jnp.bfloat16), w_embed, preferred_element_type=jnp.float32
    )
    emb = emb + root_east[..., None] * root_rows[0] + root_north[..., None] * root_rows[1]
    scale_rms = jnp.sqrt(jnp.mean(emb * emb, axis=-1, keepdims=True) + epsilon)
    return (emb / scale_rms, scale_rms)


def unit_rows(vectors):
    length = jnp.sqrt(jnp.sum(vectors * vectors, axis=-1, keepdims=True) + epsilon)
    return (vectors / length, length)


def norm_grad(grad, normed, scale_rms):
    return (grad - normed * jnp.mean(grad * normed, axis=-1, keepdims=True)) / scale_rms


def motion_grad(d_emb, normed_e, scale_rms, motion, theta, embed_rows, root_rows):
    d_unemb = norm_grad(d_emb, normed_e, scale_rms)
    d_embedded = jnp.einsum("cfd,ed->cfe", d_unemb, embed_rows, precision=highest)
    grad_east = suffix(jnp.sum(d_unemb * root_rows[0], axis=-1))
    grad_north = suffix(jnp.sum(d_unemb * root_rows[1], axis=-1))
    vel_east = motion[..., 1]
    vel_north = motion[..., 2]
    d_east, d_north = rotate(-theta, grad_east, grad_north)
    cosine = jnp.cos(theta)
    sine_term = jnp.sin(theta)
    d_theta = grad_east * (cosine * vel_north - sine_term * vel_east) - grad_north * (
        cosine * vel_east + sine_term * vel_north
    )
    d_spin = suffix(d_theta)
    return d_embedded.at[..., 0].add(d_spin).at[..., 1].add(d_east).at[..., 2].add(d_north)


def local(
    hidden,
    cond_shift,
    cond_scale,
    noisy,
    noise_level,
    w_out,
    w_embed,
    w_root,
    w_qkv,
    w_proj,
    text_table,
    text_ids,
    prompt_index,
    reward_weight,
):
    clips_dev = hidden.shape[0]
    ways = lax.axis_size("seq")
    me = lax.axis_index("seq")
    head_size = D_REW // HEADS
    root_rows = w_root.astype(jnp.float32)
    embed_rows = w_embed.astype(jnp.float32)
    vocab_rows = text_table.shape[0]
    local_ids = text_ids - me * vocab_rows
    inside = (local_ids >= 0) & (local_ids < vocab_rows)
    picked = jnp.take(text_table, jnp.clip(local_ids, 0, vocab_rows - 1), axis=0).astype(
        jnp.float32
    )
    text_part = jnp.sum(jnp.where(inside[..., None], picked, 0.0), axis=1)
    proj_dev = w_proj.shape[0]
    proj_text = lax.all_gather(
        jnp.concatenate([w_proj.astype(jnp.float32), text_part], axis=0), "seq", axis=0
    )
    proj_rows = proj_text[:, :proj_dev].reshape(ways * proj_dev, w_proj.shape[1])
    text_raw = jnp.sum(proj_text[:, proj_dev:], axis=0)
    text_unit, text_len = unit_rows(text_raw)
    w_all = lax.all_gather(w_qkv, "seq", axis=0)
    hidden_f = hidden.astype(jnp.float32)
    centred = hidden_f - jnp.mean(hidden_f, axis=-1, keepdims=True)
    inv_std = lax.rsqrt(jnp.mean(centred * centred, axis=-1, keepdims=True) + epsilon)
    normed_h = centred * inv_std
    gain = 1.0 + cond_scale.astype(jnp.float32)[:, None, :]
    modulated = (normed_h * gain + cond_shift.astype(jnp.float32)[:, None, :]).astype(jnp.bfloat16)
    eps_pred = jnp.einsum("cfd,de->cfe", modulated, w_out, preferred_element_type=jnp.float32)
    level = noise_level[:, None, None]
    x_clean = noisy.astype(jnp.float32) - level * eps_pred
    theta, path_east, path_north = local_path(x_clean)
    normed_e, scale_rms = embed(x_clean, path_east, path_north, w_embed, root_rows)
    projected = jnp.einsum(
        "cfd,hjdk->cfhjk", normed_e.astype(jnp.bfloat16), w_all, preferred_element_type=jnp.float32
    )
    query_unit, query_len = unit_rows(projected[:, :, :, 0])
    key_unit, key_len = unit_rows(projected[:, :, :, 1])
    asking_vectors_group = query_unit.astype(jnp.bfloat16)
    lookup_vectors_group = key_unit.astype(jnp.bfloat16)
    value_b = projected[:, :, :, 2].astype(jnp.bfloat16)
    similarity_table = normalizing_sharpness * jnp.einsum(
        "cfhd,cghd->chfg",
        asking_vectors_group,
        lookup_vectors_group,
        preferred_element_type=jnp.float32,
    )
    expo = jnp.exp(similarity_table)
    focus_probabilities = expo / jnp.sum(expo, axis=-1, keepdims=True)
    attention_b = focus_probabilities.astype(jnp.bfloat16)
    column_mass = jnp.sum(attention_b, axis=2, dtype=jnp.float32)
    value_f = value_b.astype(jnp.float32)
    pooled = jnp.einsum("chg,cghd->chd", column_mass, value_f, precision=highest)
    pooled_b = pooled.astype(jnp.bfloat16).reshape(clips_dev, D_REW)
    motion_emb = jnp.dot(
        pooled_b, proj_rows.astype(jnp.bfloat16), preferred_element_type=jnp.float32
    )
    prompts = lax.dynamic_slice_in_dim(prompt_index, me * clips_dev, clips_dev)
    weights = lax.dynamic_slice_in_dim(reward_weight, me * clips_dev, clips_dev)
    choose = (prompts[:, None] == jnp.arange(PROMPTS)[None, :]).astype(jnp.float32)
    target = jnp.dot(choose, text_unit, precision=highest)
    emb_len = jnp.sqrt(jnp.sum(motion_emb * motion_emb, axis=-1) + epsilon)
    rewards = jnp.sum(motion_emb * target, axis=-1) / emb_len
    d_memb = (
        (-weights)[:, None]
        * (target - rewards[:, None] * motion_emb / emb_len[:, None])
        / emb_len[:, None]
    )
    d_pooled = jnp.dot(d_memb, proj_rows.T, precision=highest).reshape(clips_dev, HEADS, head_size)
    reduction_dimension = jnp.einsum("chd,cghd->chg", d_pooled, value_f, precision=highest)
    d_value = jnp.transpose(column_mass, (0, 2, 1))[..., None] * d_pooled[:, None]
    pairwise_dot_similarity = jnp.sum(
        focus_probabilities * reduction_dimension[:, :, None, :], axis=-1, keepdims=True
    )
    similarity_derivative = (
        normalizing_sharpness
        * focus_probabilities
        * (reduction_dimension[:, :, None, :] - pairwise_dot_similarity)
    ).astype(jnp.bfloat16)
    d_qu = jnp.einsum(
        "chfg,cghd->cfhd",
        similarity_derivative,
        lookup_vectors_group,
        preferred_element_type=jnp.float32,
    )
    d_ku = jnp.einsum(
        "chfg,cfhd->cghd",
        similarity_derivative,
        asking_vectors_group,
        preferred_element_type=jnp.float32,
    )
    d_query = (d_qu - query_unit * jnp.sum(query_unit * d_qu, axis=-1, keepdims=True)) / query_len
    d_key = (d_ku - key_unit * jnp.sum(key_unit * d_ku, axis=-1, keepdims=True)) / key_len
    d_proj = jnp.stack([d_query, d_key, d_value], axis=3).astype(jnp.bfloat16)
    d_emb = jnp.einsum("cfhjk,hjdk->cfd", d_proj, w_all, preferred_element_type=jnp.float32)
    d_motion = motion_grad(d_emb, normed_e, scale_rms, x_clean, theta, embed_rows, root_rows)
    d_eps_b = (-level * d_motion).astype(jnp.bfloat16)
    d_mod = jnp.einsum("cfe,de->cfd", d_eps_b, w_out, preferred_element_type=jnp.float32)
    d_norm = d_mod * gain
    grad_hidden = (
        inv_std
        * (
            d_norm
            - jnp.mean(d_norm, axis=-1, keepdims=True)
            - normed_h * jnp.mean(d_norm * normed_h, axis=-1, keepdims=True)
        )
    ).astype(jnp.bfloat16)
    grad_term = jnp.einsum("cfd,cfe->de", modulated, d_eps_b, preferred_element_type=jnp.float32)
    rows_dev = w_out.shape[0] // ways
    cols = grad_term.shape[1]
    n_dp = lax.axis_size("dp")
    total_clips = clips_dev * ways * n_dp * lax.axis_size("sec")
    extra = -(-total_clips // cols)
    extra = -(-extra // 8) * 8
    first_clip = ((lax.axis_index("sec") * n_dp + lax.axis_index("dp")) * ways + me) * clips_dev
    columns = jnp.arange(extra * cols)
    slots = columns[None, :] == (first_clip + jnp.arange(clips_dev))[:, None]
    reward_rows = jnp.sum(jnp.where(slots, rewards[:, None], 0.0), axis=0).reshape(extra, cols)
    stacked = jnp.concatenate(
        [
            grad_term.reshape(ways, rows_dev, cols),
            jnp.broadcast_to(reward_rows[None], (ways, extra, cols)),
        ],
        axis=1,
    ).reshape(ways * (rows_dev + extra), cols)
    block = lax.psum_scatter(stacked, "seq", scatter_dimension=0, tiled=True)
    block = lax.psum(block, ("sec", "dp"))
    grad_w_out = block[:rows_dev]
    group_first = (lax.axis_index("sec") * n_dp + lax.axis_index("dp")) * ways * clips_dev
    all_rewards = block[rows_dev:].reshape(extra * cols)
    rewards_out = lax.dynamic_slice_in_dim(all_rewards, group_first, ways * clips_dev)
    return (rewards_out, grad_w_out, grad_hidden)


def solution(mesh):
    placed = (
        P(("sec", "dp", "seq"), None, None),
        P(("sec", "dp", "seq"), None),
        P(("sec", "dp", "seq"), None),
        P(("sec", "dp", "seq"), None, None),
        P(("sec", "dp", "seq")),
        P(),
        P(),
        P(),
        P(None, None, "seq"),
        P("seq", None),
        P("seq", None),
        P(),
        P(("sec", "dp")),
        P(("sec", "dp")),
    )
    return jax.shard_map(
        local,
        mesh=mesh,
        in_specs=placed,
        out_specs=(P(("sec", "dp")), P("seq", None), P(("sec", "dp", "seq"), None, None)),
        check_vma=False,
    )
```

profile of v0, /device:TPU:32, one launch (start us, length us, event | category | flops | bytes accessed | tf_op | source)
XLA Modules:
  0.0 444.6 jit_solution(8635623600535376236)
XLA Ops:
  7.2 0.9 compare_and_fusion
  8.2 0.9 convert_element_type.93
  9.1 5.1 %gather_fusion = bf16[1024,512]{1,0:T(8,128)(2,1)} fusion(bf16[3088,512]{1,0:T(8,128)(2,1)S(1)} %copy-done, s32[1024]{0:T(1024)S(1)} %broadcast_clamp_fusion), kind=kCustom, calls=%fused_computation | custom fusion | bytes 2101248 | tf_op jit(solution)/shard_map/jit(_take)/gather | solution.py:93
  14.2 1.6 select_reduce_fusion
  15.9 0.7 pad_maximum_fusion.2
  16.7 0.7 all-gather.5.cloned.1.call-update
  18.1 0.6 dynamic_slice.9
  19.4 0.6 dynamic_slice.10
  20.1 1.3 convert_reduce_fusion
  21.4 1.4 fusion.19
  22.8 2.0 fusion.21
  24.8 0.8 slice_reduce_fusion.2
  27.5 0.8 reduce_window_sum.36
  28.4 1.0 subtract_reduce_fusion
  29.3 0.8 fusion.65
  30.1 2.7 multiply_reduce_fusion.4
  32.8 29.8 %all-gather.7.cloned.1.call-done = f32[2560,512]{1,0:T(8,128)} async-done(((f32[160,512]{1,0:T(8,128)}), f32[2560,512]{1,0:T(8,128)}) %all-gather.7.cloned.1.call-update) | async-done | bytes 5242896 | tf_op jit(solution)/shard_map/all_gather | solution.py:98
  62.6 1.3 slice_reduce_fusion
  64.1 0.9 fusion.42
  64.9 131.2 %all-gather.5.cloned.1.call-done = bf16[48,2048,128]{2,1,0:T(8,128)(2,1)} async-done(((bf16[3,2048,128]{2,1,0:T(8,128)(2,1)}), bf16[48,2048,128]{2,1,0:T(8,128)(2,1)}) %all-gather.5.cloned.1.call-update) | async-done | bytes 25165840 | tf_op jit(solution)/shard_map/all_gather | solution.py:104
  196.1 16.0 %convolution_bitcast_fusion.1 = f32[1,128,16,3,128]{1,4,3,2,0:T(8,128)} fusion(bf16[16,3,2048,128]{3,2,1,0:T(8,128)(2,1)} %bitcast.182, f32[128,2048]{1,0:T(8,128)} %get-tuple-element.74, f32[128]{0:T(128)S(1)} %add_sqrt_fusion.3), kind=kOutput, calls=%fused_computation.12 | convolution fusion | flops 3221749760 | bytes 29360640 | tf_op jit(solution)/shard_map/cfd,hjdk->cfhjk/dot_general | solution.py:116
  212.2 1.7 fusion.22
  213.9 2.8 fusion.23
  216.7 2.7 convert_reduce_fusion.1
  219.4 2.1 fusion.34
  221.5 2.6 fusion.4
  224.1 0.6 multiply_reduce_fusion.10
  226.1 5.4 %fusion.1 = f32[1,16,128]{2,0,1:T(1,128)S(1)} fusion(f32[512,1,1]{0,1,2:T(1,128)S(1)} %bitcast.203, f32[16,160,512]{2,1,0:T(8,128)} %bitcast.186), kind=kOutput, calls=%fused_computation.2 | convolution fusion | flops 12582912 | bytes 4204544 | tf_op jit(solution)/shard_map/dot_general | solution.py:151
  231.5 0.6 fusion.47
  234.2 0.8 multiply_reduce_fusion.2
  234.9 1.1 multiply_convert_fusion
  236.1 1.6 fusion.30
  237.6 14.5 %multiply_reduce_fusion = (f32[128]{0:T(128)S(1)}, f32[128,2048]{1,0:T(8,128)}) fusion(f32[128,2048]{1,0:T(8,128)} %get-tuple-element.74, f32[128]{0:T(128)S(1)} %add_sqrt_fusion.3, bf16[16,3,2048,128]{3,2,1,0:T(8,128)(2,1)} %bitcast.183, bf16[128,16,1,128]{0,3,1,2:T(8,128)(2,1)} %multiply_convert_fusion, bf16[128,16,1,128]{0,3,1,2:T(8,128)(2,1)} %get-tuple-element.60, ...), kind=kOutput, calls=%fused_computation.50 | convolution fusion | flops 3223584768 | bytes 28836864 | tf_op jit(solution)/shard_map/cfhjk,hjdk->cfd/dot_general | solution.py:177
  252.2 3.7 multiply_reduce_fusion.8
  256.5 1.9 fusion.56
  258.8 2.7 fusion.66
  261.5 1.3 fusion.36
  262.8 1.0 scatter-add.10
  265.2 3.2 fusion.15
  268.4 1.5 reduce_sum.241
  269.9 3.1 fusion.18
  273.0 2.2 copy.68
  275.2 1.6 fusion.37
  276.8 1.8 pad_maximum_fusion
  278.7 57.8 %reduce-scatter.2.cloned.1.call-done = f32[168,256]{1,0:T(8,128)} async-done(((f32[2688,256]{1,0:T(8,128)}), f32[168,256]{1,0:T(8,128)}) %reduce-scatter.2.cloned.1.call-update) | async-done | bytes 172048 | tf_op jit(solution)/shard_map/reduce_scatter | solution.py:208
  336.6 98.6 %all-reduce.2.cloned.1.call-done = f32[168,256]{1,0:T(8,128)} async-done(((f32[168,256]{1,0:T(8,128)}), f32[168,256]{1,0:T(8,128)}) %all-reduce.2.cloned.1.call-update) | async-done | bytes 172048 | tf_op jit(solution)/shard_map/psum | solution.py:209
  435.2 0.7 slice_bitcast_fusion.1
  436.5 1.6 slice.138
  (106 shorter events, 7.5 us)
Async XLA Ops:
  7.2 2.0 copy-start
  7.2 55.4 %all-gather.7.cloned.1.call-start = ((), (), s32[]{:S(2)}) async-start(), calls=%async_computation.4 | async-start | bytes 5570560 | tf_op jit(solution)/shard_map/all_gather | solution.py:98
  15.8 2.3 copy-start.29
  15.9 3.5 copy-start.30
  15.9 4.1 copy-start.16
  15.9 4.1 copy-start.17
  16.6 6.2 %copy-start.28 = (bf16[1,128,256]{2,1,0:T(8,128)(2,1)S(1)}, bf16[1,128,256]{2,1,0:T(8,128)(2,1)}, u32[]{:S(2)}) copy-start(bf16[1,128,256]{2,1,0:T(8,128)(2,1)} %param.23) | copy-start | bytes 196612
  16.7 179.5 %all-gather.5.cloned.1.call-start = ((), (), s32[]{:S(2)}) async-start(), calls=%async_computation.3 | async-start | bytes 26738688 | tf_op jit(solution)/shard_map/all_gather | solution.py:104
  17.4 319.1 %reduce-scatter.2.cloned.1.call-start = ((), (), s32[]{:S(2)}) async-start(), calls=%async_computation.1 | async-start | bytes 2924544 | tf_op jit(solution)/shard_map/reduce_scatter | solution.py:208
  20.1 4.7 %copy-start.7 = (f32[2560]{0:T(1024)}, f32[2560]{0:T(1024)S(1)}, u32[]{:S(2)}) copy-start(f32[2560]{0:T(1024)S(1)} %get-tuple-element.83) | copy-start | bytes 30724
  20.1 4.7 %copy-start.9 = (f32[2560]{0:T(1024)}, f32[2560]{0:T(1024)S(1)}, u32[]{:S(2)}) copy-start(f32[2560]{0:T(1024)S(1)} %get-tuple-element.82) | copy-start | bytes 30724
  21.4 3.4 copy-start.18
  22.8 2.8 copy-start.26
  25.6 0.6 copy-start.22
  26.1 0.6 copy-start.24
  27.3 36.6 %copy-start.4 = (f32[1,128,1]{2,1,0:T(8,128)}, f32[1,128,1]{2,1,0:T(8,128)S(1)}, u32[]{:S(2)}) copy-start(f32[1,128,1]{2,1,0:T(8,128)S(1)} %get-tuple-element.66) | copy-start | bytes 1540
  30.1 32.5 %copy-start.11 = (f32[1,2048]{1,0:T(1,128)}, f32[1,2048]{1,0:T(1,128)S(1)}, u32[]{:S(2)}) copy-start(f32[1,2048]{1,0:T(1,128)S(1)} %get-tuple-element.68) | copy-start | bytes 24580
  30.1 32.5 %copy-start.13 = (f32[1,2048]{1,0:T(1,128)}, f32[1,2048]{1,0:T(1,128)S(1)}, u32[]{:S(2)}) copy-start(f32[1,2048]{1,0:T(1,128)S(1)} %get-tuple-element.69) | copy-start | bytes 24580
  226.1 6.1 %copy-start.1 = (f32[1,128,16,3,128]{1,4,3,2,0:T(8,128)S(1)}, f32[1,128,16,3,128]{1,4,3,2,0:T(8,128)}, u32[]{:S(2)}) copy-start(f32[1,128,16,3,128]{1,4,3,2,0:T(8,128)} %convolution_bitcast_fusion.1) | copy-start | bytes 9437188
  231.5 1.2 copy-start.2
  231.5 1.6 copy-start.3
  233.1 1.0 copy-start.6
  237.6 14.5 %copy-start.12 = (f32[1,2048]{1,0:T(1,128)S(1)}, f32[1,2048]{1,0:T(1,128)}, u32[]{:S(2)}) copy-start(f32[1,2048]{1,0:T(1,128)} %copy-done.11) | copy-start | bytes 24580
  237.6 14.5 %copy-start.14 = (f32[1,2048]{1,0:T(1,128)S(1)}, f32[1,2048]{1,0:T(1,128)}, u32[]{:S(2)}) copy-start(f32[1,2048]{1,0:T(1,128)} %copy-done.13) | copy-start | bytes 24580
  252.1 4.3 copy-start.20
  252.1 4.3 copy-start.21
  252.1 4.3 copy-start.23
  252.1 4.3 copy-start.25
  252.1 6.5 %copy-start.5 = (f32[1,128,1]{2,1,0:T(8,128)S(1)}, f32[1,128,1]{2,1,0:T(8,128)}, u32[]{:S(2)}) copy-start(f32[1,128,1]{2,1,0:T(8,128)} %copy-done.4) | copy-start | bytes 1540
  265.1 4.7 %copy-start.8 = (f32[2560]{0:T(1024)S(1)}, f32[2560]{0:T(1024)}, u32[]{:S(2)}) copy-start(f32[2560]{0:T(1024)} %copy-done.7) | copy-start | bytes 30724
  265.2 4.7 %copy-start.10 = (f32[2560]{0:T(1024)S(1)}, f32[2560]{0:T(1024)}, u32[]{:S(2)}) copy-start(f32[2560]{0:T(1024)} %copy-done.9) | copy-start | bytes 30724
  265.2 4.7 %copy-start.19 = (f32[128]{0:T(128)S(1)}, f32[128]{0:T(128)}, u32[]{:S(2)}) copy-start(f32[128]{0:T(128)} %copy-done.18) | copy-start | bytes 1540
  265.2 4.7 %copy-start.27 = (f32[128]{0:T(128)S(1)}, f32[128]{0:T(128)}, u32[]{:S(2)}) copy-start(f32[128]{0:T(128)} %copy-done.26) | copy-start | bytes 1540
  275.2 1.6 copy-start.15
  278.6 156.6 %all-reduce.2.cloned.1.call-start = ((), (), s32[]{:S(2)}) async-start(), calls=%async_computation.2 | async-start | bytes 344064 | tf_op jit(solution)/shard_map/psum | solution.py:209
Sparse Core Ops, SparseCore 0:
  16.8 45.7 all-gather.6
  64.4 131.6 all-gather.4
  278.8 57.7 reduce-scatter.1
  340.0 95.2 all-reduce.1
where the time goes:
time: 446 us; the launch traced here: 445 us
  waiting for transfers between devices  318 us (71%)
  matrix products  58.1 us (13%)
  other arithmetic  34.6 us (8%)
  between operations  16.9 us (4%)
  local copies, waits for them, and re-layouts  16.6 us (4%)
    all_gather x1, waiting for transfers between devices, local(): w_all = lax.all_gather(w_qkv, 'seq', axis=0)  131 us
    psum x1, waiting for transfers between devices, local(): block = lax.psum(block, ('sec', 'dp'))  98.6 us
    reduce_scatter x1, waiting for transfers between devices, local(): block = lax.psum_scatter(stacked, 'seq', scatter_dimension=0, tiled=True)  57.8 us
    all_gather x1, waiting for transfers between devices, local(): lax.all_gather(jnp.concatenate([w_proj.astype(jnp.float32), text_part], a...  29.8 us
    dot_general x1, matrix products, local(): jnp.einsum('cfd,hjdk->cfhjk', normed_e.astype(jnp.bfloat16), w_all, prefe...  16 us
    dot_general x1, matrix products, local(): jnp.einsum('cfhjk,hjdk->cfd', d_proj, w_all, preferred_element_type=jnp.f...  14.5 us
  transfers between devices with their start and end apart: 4, of which 4 were waited for; matrix products, arithmetic and copies ran while one was open for 3% of the time, Pallas kernels for 0%

commit v1 on v0

--- a/solution.py
+++ b/solution.py
@@ -206,7 +206,8 @@
         axis=1,
     ).reshape(ways * (rows_dev + extra), cols)
     block = lax.psum_scatter(stacked, "seq", scatter_dimension=0, tiled=True)
-    block = lax.psum(block, ("sec", "dp"))
+    for mesh_axis in ("sec", "dp"):
+        block = lax.psum(block, mesh_axis)
     grad_w_out = block[:rows_dev]
     group_first = (lax.axis_index("sec") * n_dp + lax.axis_index("dp")) * ways * clips_dev
     all_rewards = block[rows_dev:].reshape(extra * cols)

time: 446 us -> 477 us (1.070)
  waiting for transfers between devices: 318 us -> 349 us
    psum x1 -> x2, waiting for transfers between devices: 98.6 us -> 130 us  [local(): block = lax.psum(block, mesh_axis)]
  transfers between devices with their start and end apart: 4 -> 5, of which waited for: 4 -> 5; matrix products, arithmetic and copies ran while one was open for 3% -> 3% of each run, Pallas kernels for 0% -> 0%
where the time goes in v1:
time: 477 us; the launch traced here: 476 us
  waiting for transfers between devices  349 us (73%)
  matrix products  58.1 us (12%)
  other arithmetic  34.6 us (7%)
  between operations  16.9 us (4%)
  local copies, waits for them, and re-layouts  16.6 us (3%)
    all_gather x1, waiting for transfers between devices, local(): w_all = lax.all_gather(w_qkv, 'seq', axis=0)  131 us
    psum x2, waiting for transfers between devices, local(): block = lax.psum(block, mesh_axis)  130 us
    reduce_scatter x1, waiting for transfers between devices, local(): block = lax.psum_scatter(stacked, 'seq', scatter_dimension=0, tiled=True)  57.8 us
    all_gather x1, waiting for transfers between devices, local(): lax.all_gather(jnp.concatenate([w_proj.astype(jnp.float32), text_part], a...  29.8 us
    dot_general x1, matrix products, local(): jnp.einsum('cfd,hjdk->cfhjk', normed_e.astype(jnp.bfloat16), w_all, prefe...  16 us
    dot_general x1, matrix products, local(): jnp.einsum('cfhjk,hjdk->cfd', d_proj, w_all, preferred_element_type=jnp.f...  14.5 us
  transfers between devices with their start and end apart: 5, of which 5 were waited for; matrix products, arithmetic and copies ran while one was open for 3% of the time, Pallas kernels for 0%

profile of v1, /device:TPU:32, one launch (start us, length us, event | category | flops | bytes accessed | tf_op | source)
XLA Modules:
  0.0 475.8 jit_solution(4514642923485365420)
XLA Ops:
  7.2 0.9 compare_and_fusion
  8.2 0.9 convert_element_type.93
  9.1 5.1 %gather_fusion = bf16[1024,512]{1,0:T(8,128)(2,1)} fusion(bf16[3088,512]{1,0:T(8,128)(2,1)S(1)} %copy-done, s32[1024]{0:T(1024)S(1)} %broadcast_clamp_fusion), kind=kCustom, calls=%fused_computation | custom fusion | bytes 2101248 | tf_op jit(solution)/shard_map/jit(_take)/gather | solution.py:93
  14.2 1.6 select_reduce_fusion
  15.9 0.7 pad_maximum_fusion.2
  16.7 0.7 all-gather.5.cloned.1.call-update
  19.4 0.6 dynamic_slice.10
  20.1 1.3 convert_reduce_fusion
  21.4 1.4 fusion.19
  22.8 2.0 fusion.21
  24.8 0.8 slice_reduce_fusion.2
  27.5 0.8 reduce_window_sum.36
  28.4 1.0 subtract_reduce_fusion
  29.3 0.8 fusion.65
  30.1 2.7 multiply_reduce_fusion.4
  32.8 29.8 %all-gather.7.cloned.1.call-done = f32[2560,512]{1,0:T(8,128)} async-done(((f32[160,512]{1,0:T(8,128)}), f32[2560,512]{1,0:T(8,128)}) %all-gather.7.cloned.1.call-update) | async-done | bytes 5242896 | tf_op jit(solution)/shard_map/all_gather | solution.py:98
  62.6 1.3 slice_reduce_fusion
  64.1 0.9 fusion.42
  64.9 131.2 %all-gather.5.cloned.1.call-done = bf16[48,2048,128]{2,1,0:T(8,128)(2,1)} async-done(((bf16[3,2048,128]{2,1,0:T(8,128)(2,1)}), bf16[48,2048,128]{2,1,0:T(8,128)(2,1)}) %all-gather.5.cloned.1.call-update) | async-done | bytes 25165840 | tf_op jit(solution)/shard_map/all_gather | solution.py:104
  196.1 16.0 %convolution_bitcast_fusion.1 = f32[1,128,16,3,128]{1,4,3,2,0:T(8,128)} fusion(bf16[16,3,2048,128]{3,2,1,0:T(8,128)(2,1)} %bitcast.182, f32[128,2048]{1,0:T(8,128)} %get-tuple-element.74, f32[128]{0:T(128)S(1)} %add_sqrt_fusion.3), kind=kOutput, calls=%fused_computation.12 | convolution fusion | flops 3221749760 | bytes 29360640 | tf_op jit(solution)/shard_map/cfd,hjdk->cfhjk/dot_general | solution.py:116
  212.2 1.7 fusion.22
  213.9 2.8 fusion.23
  216.7 2.7 convert_reduce_fusion.1
  219.4 2.1 fusion.34
  221.5 2.6 fusion.4
  224.1 0.6 multiply_reduce_fusion.10
  226.1 5.4 %fusion.1 = f32[1,16,128]{2,0,1:T(1,128)S(1)} fusion(f32[512,1,1]{0,1,2:T(1,128)S(1)} %bitcast.203, f32[16,160,512]{2,1,0:T(8,128)} %bitcast.186), kind=kOutput, calls=%fused_computation.2 | convolution fusion | flops 12582912 | bytes 4204544 | tf_op jit(solution)/shard_map/dot_general | solution.py:151
  231.5 0.6 fusion.47
  234.2 0.8 multiply_reduce_fusion.2
  234.9 1.1 multiply_convert_fusion
  236.1 1.6 fusion.30
  237.6 14.5 %multiply_reduce_fusion = (f32[128]{0:T(128)S(1)}, f32[128,2048]{1,0:T(8,128)}) fusion(f32[128,2048]{1,0:T(8,128)} %get-tuple-element.74, f32[128]{0:T(128)S(1)} %add_sqrt_fusion.3, bf16[16,3,2048,128]{3,2,1,0:T(8,128)(2,1)} %bitcast.183, bf16[128,16,1,128]{0,3,1,2:T(8,128)(2,1)} %multiply_convert_fusion, bf16[128,16,1,128]{0,3,1,2:T(8,128)(2,1)} %get-tuple-element.60, ...), kind=kOutput, calls=%fused_computation.50 | convolution fusion | flops 3223584768 | bytes 28836864 | tf_op jit(solution)/shard_map/cfhjk,hjdk->cfd/dot_general | solution.py:177
  252.2 3.7 multiply_reduce_fusion.8
  256.5 1.9 fusion.56
  258.8 2.7 fusion.66
  261.5 1.3 fusion.36
  262.8 1.0 scatter-add.10
  265.2 3.2 fusion.15
  268.4 1.5 reduce_sum.241
  269.9 3.1 fusion.18
  273.0 2.2 copy.68
  275.2 1.6 fusion.37
  276.8 1.8 pad_maximum_fusion
  278.7 57.8 %reduce-scatter.2.cloned.1.call-done = f32[168,256]{1,0:T(8,128)} async-done(((f32[2688,256]{1,0:T(8,128)}), f32[168,256]{1,0:T(8,128)}) %reduce-scatter.2.cloned.1.call-update) | async-done | bytes 172048 | tf_op jit(solution)/shard_map/reduce_scatter | solution.py:208
  336.6 38.0 %all-reduce.3.cloned.1.call-done = f32[168,256]{1,0:T(8,128)} async-done(((f32[168,256]{1,0:T(8,128)}), f32[168,256]{1,0:T(8,128)}) %all-reduce.3.cloned.1.call-update) | async-done | bytes 172048 | tf_op jit(solution)/shard_map/psum | solution.py:210
  374.6 91.7 %all-reduce.5.cloned.1.call-done = f32[168,256]{1,0:T(8,128)} async-done(((f32[168,256]{1,0:T(8,128)}), f32[168,256]{1,0:T(8,128)}) %all-reduce.5.cloned.1.call-update) | async-done | bytes 172048 | tf_op jit(solution)/shard_map/psum | solution.py:210
  466.4 0.7 slice_bitcast_fusion.1
  467.7 1.6 slice.138
  (109 shorter events, 8.2 us)
Async XLA Ops:
  7.2 2.0 copy-start
  7.2 55.4 %all-gather.7.cloned.1.call-start = ((), (), s32[]{:S(2)}) async-start(), calls=%async_computation.5 | async-start | bytes 5570560 | tf_op jit(solution)/shard_map/all_gather | solution.py:98
  15.8 2.3 copy-start.29
  15.9 3.5 copy-start.30
  15.9 4.1 copy-start.16
  15.9 4.1 copy-start.17
  16.6 6.2 %copy-start.28 = (bf16[1,128,256]{2,1,0:T(8,128)(2,1)S(1)}, bf16[1,128,256]{2,1,0:T(8,128)(2,1)}, u32[]{:S(2)}) copy-start(bf16[1,128,256]{2,1,0:T(8,128)(2,1)} %param.23) | copy-start | bytes 196612
  16.7 179.5 %all-gather.5.cloned.1.call-start = ((), (), s32[]{:S(2)}) async-start(), calls=%async_computation.4 | async-start | bytes 26738688 | tf_op jit(solution)/shard_map/all_gather | solution.py:104
  17.4 319.1 %reduce-scatter.2.cloned.1.call-start = ((), (), s32[]{:S(2)}) async-start(), calls=%async_computation.1 | async-start | bytes 2924544 | tf_op jit(solution)/shard_map/reduce_scatter | solution.py:208
  20.1 4.7 copy-start.7
  20.1 4.7 copy-start.9
  21.4 3.4 copy-start.18
  22.8 2.8 copy-start.26
  25.6 0.6 copy-start.22
  26.1 0.6 copy-start.24
  27.3 36.6 %copy-start.4 = (f32[1,128,1]{2,1,0:T(8,128)}, f32[1,128,1]{2,1,0:T(8,128)S(1)}, u32[]{:S(2)}) copy-start(f32[1,128,1]{2,1,0:T(8,128)S(1)} %get-tuple-element.66) | copy-start | bytes 1540
  30.1 32.5 %copy-start.11 = (f32[1,2048]{1,0:T(1,128)}, f32[1,2048]{1,0:T(1,128)S(1)}, u32[]{:S(2)}) copy-start(f32[1,2048]{1,0:T(1,128)S(1)} %get-tuple-element.68) | copy-start | bytes 24580
  30.1 32.5 %copy-start.13 = (f32[1,2048]{1,0:T(1,128)}, f32[1,2048]{1,0:T(1,128)S(1)}, u32[]{:S(2)}) copy-start(f32[1,2048]{1,0:T(1,128)S(1)} %get-tuple-element.69) | copy-start | bytes 24580
  226.1 6.1 %copy-start.1 = (f32[1,128,16,3,128]{1,4,3,2,0:T(8,128)S(1)}, f32[1,128,16,3,128]{1,4,3,2,0:T(8,128)}, u32[]{:S(2)}) copy-start(f32[1,128,16,3,128]{1,4,3,2,0:T(8,128)} %convolution_bitcast_fusion.1) | copy-start | bytes 9437188
  231.5 1.2 copy-start.2
  231.5 1.6 copy-start.3
  233.1 1.0 copy-start.6
  237.6 14.5 %copy-start.12 = (f32[1,2048]{1,0:T(1,128)S(1)}, f32[1,2048]{1,0:T(1,128)}, u32[]{:S(2)}) copy-start(f32[1,2048]{1,0:T(1,128)} %copy-done.11) | copy-start | bytes 24580
  237.6 14.5 %copy-start.14 = (f32[1,2048]{1,0:T(1,128)S(1)}, f32[1,2048]{1,0:T(1,128)}, u32[]{:S(2)}) copy-start(f32[1,2048]{1,0:T(1,128)} %copy-done.13) | copy-start | bytes 24580
  252.1 4.3 copy-start.20
  252.1 4.3 copy-start.21
  252.1 4.3 copy-start.23
  252.1 4.3 copy-start.25
  252.1 6.5 %copy-start.5 = (f32[1,128,1]{2,1,0:T(8,128)S(1)}, f32[1,128,1]{2,1,0:T(8,128)}, u32[]{:S(2)}) copy-start(f32[1,128,1]{2,1,0:T(8,128)} %copy-done.4) | copy-start | bytes 1540
  265.1 4.7 copy-start.8
  265.2 4.7 copy-start.10
  265.2 4.7 copy-start.19
  265.2 4.7 copy-start.27
  275.2 1.6 copy-start.15
  278.6 96.0 %all-reduce.3.cloned.1.call-start = ((), (), s32[]{:S(2)}) async-start(), calls=%async_computation.2 | async-start | bytes 344064 | tf_op jit(solution)/shard_map/psum | solution.py:210
  336.6 129.8 %all-reduce.5.cloned.1.call-start = ((), (), s32[]{:S(2)}) async-start(), calls=%async_computation.3 | async-start | bytes 344064 | tf_op jit(solution)/shard_map/psum | solution.py:210
Sparse Core Ops, SparseCore 0:
  16.8 45.7 all-gather.6
  64.4 131.6 all-gather.4
  278.8 57.7 reduce-scatter.1
  339.1 35.4 all-reduce.2
  377.3 89.0 all-reduce.4
